TPU v7x, 256 devices: a whole 4x4x8 slice. The times are simulated.
256 devices in a mesh: frame: 16 (over z_lo, y), tensor: 8 (over z_hi, x), dp: 2 (over core).
Axes of the slice: x: 4, y: 4, z: 8 (z_hi: 2, z_lo: 4; z = z_hi * 4 + z_lo), core: 2. Of those that a mesh axis runs over, the one named last changes fastest.
Arguments:
- q_proj: bfloat16 [16384, 3072], P(('dp', 'frame'), 'tensor'), parts along dimension 0
- k_proj: bfloat16 [16384, 3072], P(('dp', 'frame'), 'tensor'), parts along dimension 0
- v_proj: bfloat16 [16384, 3072], P(('dp', 'frame'), 'tensor'), parts along dimension 0, may hold values from -6 to 6
- gain_q: float32 [3072], P('tensor'), may hold values from 0.5 to 6
- gain_k: float32 [3072], P('tensor'), may hold values from 0.5 to 6
- tiles: int32 [128, 12], P('dp'), parts along dimension 0, may hold values from 0 to 63, as said below
Outputs:
- attended: bfloat16 [16384, 3072], P(('dp', 'frame'), 'tensor'), parts along dimension 0
There are 2 independent parts, one for each index of `dp`. A program takes and returns all parts, laid end to end along the dimension named above; an argument that names none is the same for every part. Nothing has to cross between parts.
Inputs may be any that keep to these rules, and one draw needn't show every extreme that they name: `tiles`: row q lists 12 distinct key blocks: q first; then 8 blocks whose slab (group of 4 consecutive blocks, one frame slab) is at most 2 slabs from the slab of q; then 3 blocks that are each the first block of a slab more than 2 slabs away. Farther groups are listed less often.
All inputs are finite; a program needn't handle non-finite values.
Results may differ from a plain program's by a relative error of at most 0.007.
The roundings to bfloat16 on the way count: a program that leaves them out, or rounds other values in their place, can miss the bound.
Values may be sent and summed in bfloat16 or wider, within the bound.
No kernel may reach another device: no remote copies, remote signals or barrier semaphores. Data moves between devices by JAX's collectives and lax.ppermute only.
A program may use at most 128 MiB of HBM per device.

v0:
```python
import math
import jax
import jax.numpy as jnp
from jax import lax
from jax.sharding import PartitionSpec as P

HD = 128
BLK = 128
EPS = 1e-06


def attend(state_now, q_heads, keys, values, key_ids, q_tiles):
    run_max, run_sum, run_acc = state_now
    head_count = run_max.shape[0]
    tok_rows = q_heads.shape[0]
    length = keys.shape[0]
    k_heads = keys.reshape(length, head_count, HD)
    v_heads = values.reshape(length, head_count, HD)
    scores = jnp.einsum("qhd,khd->hqk", q_heads, k_heads, preferred_element_type=jnp.float32) * (
        1.0 / math.sqrt(HD)
    )
    listed = jnp.any(q_tiles[:, :, None] == key_ids[None, None, :], axis=1)
    listed = jnp.repeat(listed, tok_rows // q_tiles.shape[0], axis=0)[None]
    scores = jnp.where(listed, scores, -1e30)
    new_max = jnp.maximum(run_max, jnp.max(scores, axis=-1))
    factor = jnp.exp(run_max - new_max)
    weights = jnp.where(listed, jnp.exp(scores - new_max[..., None]), 0.0)
    new_sum = run_sum * factor + jnp.sum(weights, axis=-1)
    product = jnp.einsum(
        "hqk,khd->hqd", weights.astype(jnp.bfloat16), v_heads, preferred_element_type=jnp.float32
    )
    new_acc = run_acc * factor[..., None] + product
    return (new_max, new_sum, new_acc)


def sweep(state_now, q_heads, keys, values, key_ids, q_tiles):
    length = keys.shape[0]
    sub_rows = math.gcd(length, 512)
    steps_count = length // sub_rows
    width = keys.shape[1]
    inputs = (
        keys.reshape(steps_count, sub_rows, width),
        values.reshape(steps_count, sub_rows, width),
        key_ids.reshape(steps_count, sub_rows),
    )

    def one_step(carried, parts_now):
        return (attend(carried, q_heads, parts_now[0], parts_now[1], parts_now[2], q_tiles), None)

    final_state, unused = lax.scan(one_step, state_now, inputs)
    return final_state


def body(q_proj, k_proj, v_proj, gain_q, gain_k, tiles):
    tok_rows, width = q_proj.shape
    head_count = width // HD
    q_wide = q_proj.astype(jnp.float32)
    k_wide = k_proj.astype(jnp.float32)
    row_sums = lax.psum(
        (jnp.sum(q_wide * q_wide, axis=1), jnp.sum(k_wide * k_wide, axis=1)), "tensor"
    )
    full_width = width * lax.axis_size("tensor")
    q_norm = (q_wide * lax.rsqrt(row_sums[0] / full_width + EPS)[:, None] * gain_q).astype(
        jnp.bfloat16
    )
    k_norm = (k_wide * lax.rsqrt(row_sums[1] / full_width + EPS)[:, None] * gain_k).astype(
        jnp.bfloat16
    )
    blocks = tok_rows // BLK
    frame_pos = lax.axis_index("frame")
    q_tiles = lax.dynamic_slice_in_dim(tiles, frame_pos * blocks, blocks, 0)
    q_heads = q_norm.reshape(tok_rows, head_count, HD)
    kv_pair = jnp.stack([k_norm, v_proj])
    state_now = (
        jnp.full((head_count, tok_rows), -1e30, jnp.float32),
        jnp.zeros((head_count, tok_rows), jnp.float32),
        jnp.zeros((head_count, tok_rows, HD), jnp.float32),
    )
    portion = lax.all_gather(kv_pair, "frame", axis=1, tiled=True)
    length = portion.shape[1]
    key_ids = jnp.arange(length, dtype=jnp.int32) // BLK
    state_now = sweep(state_now, q_heads, portion[0], portion[1], key_ids, q_tiles)
    run_max, run_sum, run_acc = state_now
    result = run_acc / run_sum[..., None]
    return jnp.transpose(result, (1, 0, 2)).reshape(tok_rows, width).astype(jnp.bfloat16)


def solution(mesh):
    return jax.shard_map(
        body,
        mesh=mesh,
        in_specs=(
            P(("dp", "frame"), "tensor"),
            P(("dp", "frame"), "tensor"),
            P(("dp", "frame"), "tensor"),
            P("tensor"),
            P("tensor"),
            P("dp", None),
        ),
        out_specs=P(("dp", "frame"), "tensor"),
        check_vma=False,
    )
```

profile of v0, /device:TPU:1, one launch (start us, length us, event | category | flops | bytes accessed | tf_op | source)
XLA Modules:
  0.0 416.1 jit_solution(15182845750359665627)
XLA Ops:
  9.0 30.2 %all-reduce = (f32[512]{0:T(512)S(1)}, f32[512]{0:T(512)S(1)}) all-reduce(f32[512]{0:T(512)S(1)} %fusion.13, f32[512]{0:T(512)S(1)} %fusion.16), channel_id=1, replica_groups=mesh['frame'=16,'tensor'=8,'dp'=2] {'tensor'}, use_global_device_ids=true, to_apply=%region_1.0 | all-reduce | flops 1024 | bytes 8192 | tf_op jit(solution)/shard_map/psum | solution.py:59
  40.4 2.0 pad_maximum_fusion
  43.6 142.4 %all-gather.2.cloned.1.call-done = bf16[2,8192,384]{2,1,0:T(8,128)(2,1)} async-done(((bf16[2,512,384]{2,1,0:T(8,128)(2,1)}), bf16[2,8192,384]{2,1,0:T(8,128)(2,1)}) %all-gather.2.cloned.1.call-update) | async-done | bytes 12582928 | tf_op jit(solution)/shard_map/all_gather | solution.py:79
  186.0 10.2 %fusion.23 = (bf16[1,8192,384]{2,1,0:T(8,128)(2,1)}, bf16[1,8192,384]{2,1,0:T(8,128)(2,1)}) fusion(bf16[2,8192,384]{2,1,0:T(8,128)(2,1)} %all-gather.2.cloned.1.call-done), kind=kLoop, calls=%fused_computation.46 | loop fusion | bytes 25165824 | tf_op jit(solution)/shard_map/slice | solution.py:82
  196.2 210.6 %while.15 = (s32[]{:T(128)}, f32[3,512]{1,0:T(4,128)S(1)}, f32[3,512]{1,0:T(4,128)S(1)}, f32[3,512,128]{2,1,0:T(8,128)}, s32[4,12]{0,1:T(8,128)S(1)}, /*index=5*...) while((s32[]{:T(128)}, f32[3,512]{1,0:T(4,128)S(1)}, ...), condition=%wide.region_8.9_spmd.clone, body=%wide.region_4.8_spmd.clone.sunk | while | flops 413521408 | bytes 17021248 | solution.py:50
  201.2 2.0 fusion.39
  205.9 3.2 fusion.42
  211.2 1.9 constant_dynamic-slice_fusion.7
  214.1 2.0 fusion.39
  218.8 3.5 fusion.42
  224.4 1.9 constant_dynamic-slice_fusion.7
  227.3 2.0 fusion.39
  232.0 3.5 fusion.42
  237.6 1.9 constant_dynamic-slice_fusion.7
  240.4 2.0 fusion.39
  245.2 3.5 fusion.42
  250.7 1.9 constant_dynamic-slice_fusion.7
  253.6 2.0 fusion.39
  258.4 3.5 fusion.42
  266.8 2.0 fusion.39
  271.5 3.5 fusion.42
  277.1 1.9 constant_dynamic-slice_fusion.7
  280.0 2.0 fusion.39
  284.7 3.5 fusion.42
  290.3 1.9 constant_dynamic-slice_fusion.7
  293.2 2.0 fusion.39
  297.9 3.5 fusion.42
  306.3 2.0 fusion.39
  311.1 3.5 fusion.42
  316.6 1.9 constant_dynamic-slice_fusion.7
  319.5 2.0 fusion.39
  324.3 3.5 fusion.42
  329.8 1.9 constant_dynamic-slice_fusion.7
  332.7 2.0 fusion.39
  337.4 3.5 fusion.42
  343.0 1.9 constant_dynamic-slice_fusion.7
  345.9 2.0 fusion.39
  350.6 3.5 fusion.42
  356.2 1.9 constant_dynamic-slice_fusion.7
  359.0 2.0 fusion.39
  363.8 3.5 fusion.42
  372.2 2.0 fusion.39
  377.0 3.5 fusion.42
  385.4 2.0 fusion.39
  390.1 3.5 fusion.42
  395.7 1.9 constant_dynamic-slice_fusion.7
  398.6 2.0 fusion.39
  403.3 3.5 fusion.42
  (202 shorter events, 108.5 us)
Async XLA Ops:
  6.5 37.0 %copy-start = (s32[64,12]{0,1:T(8,128)S(1)}, s32[64,12]{0,1:T(8,128)}, u32[]{:S(2)}) copy-start(s32[64,12]{0,1:T(8,128)} %param.13) | copy-start | bytes 9220
  6.5 35.9 %copy-start.1 = (f32[384]{0:T(512)S(1)}, f32[384]{0:T(512)}, u32[]{:S(2)}) copy-start(f32[384]{0:T(512)} %param.11) | copy-start | bytes 4612
  6.5 179.4 %all-gather.2.cloned.1.call-start = ((), (), s32[]{:S(2)}) async-start(), calls=%async_computation | async-start | bytes 13369344 | tf_op jit(solution)/shard_map/all_gather | solution.py:79
Sparse Core Ops, SparseCore 0:
  42.5 143.3 all-gather.1
where the time goes:
time: 418 us; the launch traced here: 416 us
  waiting for transfers between devices  142 us (34%)
  local copies, waits for them, and re-layouts  122 us (29%)
  matrix products  87 us (21%)
  blocking collectives  30.2 us (7%)
  other arithmetic  19.6 us (5%)
  between operations  13.5 us (3%)
    all_gather x1, waiting for transfers between devices, body(): portion = lax.all_gather(kv_pair, 'frame', axis=1, tiled=True)  142 us
    dynamic_slice x64, local copies, waits for them, and re-layouts, sweep(): final_state, unused = lax.scan(one_step, state_now, inputs)  76.9 us
    dot_general x16, matrix products, attend(): jnp.einsum('hqk,khd->hqd', weights.astype(jnp.bfloat16), v_heads, preferr...  55.6 us
    dot_general x16, matrix products, attend(): jnp.einsum('qhd,khd->hqk', q_heads, k_heads, preferred_element_type=jnp.f...  31.5 us
    psum x1, blocking collectives, body(): lax.psum((jnp.sum(q_wide * q_wide, axis=1), jnp.sum(k_wide * k_wide, axis...  30.2 us
    broadcast_in_dim x16, local copies, waits for them, and re-layouts, attend(): listed = jnp.repeat(listed, tok_rows // q_tiles.shape[0], axis=0)[None]  25.6 us
    reduce_sum x16, other arithmetic, attend(): new_sum = run_sum * factor + jnp.sum(weights, axis=-1)  12.9 us
    slice x1, local copies, waits for them, and re-layouts, body(): portion[1]  10.2 us
  transfers between devices with their start and end apart: 1, of which 1 were waited for; matrix products, arithmetic and copies ran while one was open for 0% of the time, Pallas kernels for 0%

commit v1 on v0

--- a/solution.py
+++ b/solution.py
@@ -1,3 +1,4 @@
+import functools
 import math
 import jax
 import jax.numpy as jnp
@@ -7,6 +8,19 @@
 HD = 128
 BLK = 128
 EPS = 1e-06
+
+
+def raise_the_works(row_data, net_axis):
+    response = jnp.concatenate(
+        lax.all_to_all(
+            jnp.stack(tuple((row_data for _ in range(lax.axis_size(net_axis))))), net_axis, 0, 0
+        ),
+        axis=1,
+    )
+    return response
+
+
+connect_chains = functools.partial(raise_the_works, net_axis="frame")
 
 
 def attend(state_now, q_heads, keys, values, key_ids, q_tiles):
@@ -76,7 +90,7 @@
         jnp.zeros((head_count, tok_rows), jnp.float32),
         jnp.zeros((head_count, tok_rows, HD), jnp.float32),
     )
-    portion = lax.all_gather(kv_pair, "frame", axis=1, tiled=True)
+    portion = connect_chains(kv_pair)
     length = portion.shape[1]
     key_ids = jnp.arange(length, dtype=jnp.int32) // BLK
     state_now = sweep(state_now, q_heads, portion[0], portion[1], key_ids, q_tiles)

time: 418 us -> 486 us (1.16)
  the two profiles are of different devices: /device:TPU:1 before, /device:TPU:64 now
where the time goes in v1:
time: 486 us; the launch traced here: 484 us
  waiting for transfers between devices  268 us (55%)
  local copies, waits for them, and re-layouts  104 us (21%)
  matrix products  53.1 us (11%)
  blocking collectives  31.3 us (6%)
  other arithmetic  18.7 us (4%)
  starting transfers between devices  7.43 us (2%)
    all_to_all x1, waiting for transfers between devices, raise_the_works(): lax.all_to_all(jnp.stack(tuple((row_data for _ in range(lax.axis_size(net...  268 us
    psum x1, blocking collectives, body(): lax.psum((jnp.sum(q_wide * q_wide, axis=1), jnp.sum(k_wide * k_wide, axis...  31.3 us
    dynamic_slice x32, local copies, waits for them, and re-layouts, sweep(): final_state, unused = lax.scan(one_step, state_now, inputs)  30.7 us
    dot_general x16, matrix products, attend(): jnp.einsum('qhd,khd->hqk', q_heads, k_heads, preferred_element_type=jnp.f...  29.6 us
    broadcast_in_dim x16, local copies, waits for them, and re-layouts, attend(): listed = jnp.repeat(listed, tok_rows // q_tiles.shape[0], axis=0)[None]  25.6 us
    dot_general x16, matrix products, attend(): jnp.einsum('hqk,khd->hqd', weights.astype(jnp.bfloat16), v_heads, preferr...  23.6 us
    while x128, local copies, waits for them, and re-layouts  23.3 us
    reduce_sum x16, other arithmetic, attend(): new_sum = run_sum * factor + jnp.sum(weights, axis=-1)  12.9 us
  transfers between devices with their start and end apart: 1, of which 1 were waited for; matrix products, arithmetic and copies ran while one was open for 0% of the time, Pallas kernels for 0%

profile of v1, /device:TPU:64, one launch (start us, length us, event | category | flops | bytes accessed | tf_op | source)
XLA Modules:
  0.0 484.0 jit_solution(1854542131760568816)
XLA Ops:
  2.5 31.3 %all-reduce = (f32[512]{0:T(512)S(1)}, f32[512]{0:T(512)S(1)}) all-reduce(f32[512]{0:T(512)S(1)} %fusion.13, f32[512]{0:T(512)S(1)} %fusion.16), channel_id=1, replica_groups=mesh['frame'=16,'tensor'=8,'dp'=2] {'tensor'}, use_global_device_ids=true, to_apply=%region_1.0 | all-reduce | flops 1024 | bytes 8192 | tf_op jit(solution)/shard_map/psum | solution.py:73
  36.4 5.9 %stack.11 = bf16[16,2,512,384]{2,3,1,0:T(8,128)(2,1)} broadcast(bf16[2,512,384]{1,2,0:T(8,128)(2,1)S(1)} %copy.32), dimensions={1,2,3} | broadcast | bytes 13369344 | tf_op jit(solution)/shard_map/stack | solution.py:16
  42.3 7.4 %all-to-all-start = ((bf16[16,2,512,384]{2,3,1,0:T(8,128)(2,1)}), bf16[16,2,512,384]{2,3,1,0:T(8,128)(2,1)}, u32[]{:S(2)}, u32[]{:S(2)}) async-start(bf16[16,2,512,384]{2,3,1,0:T(8,128)(2,1)} %stack.11), calls=%async_computation | async-start | bytes 25165824 | tf_op jit(solution)/shard_map/all_to_all | solution.py:15
  50.9 268.1 %all-to-all-done = bf16[16,2,512,384]{2,3,1,0:T(8,128)(2,1)} async-done(((bf16[16,2,512,384]{2,3,1,0:T(8,128)(2,1)}), bf16[16,2,512,384]{2,3,1,0:T(8,128)(2,1)}, u32[]{:S(2)}, u32[]{:S(2)}) %all-to-all-start) | async-done | bytes 12582944 | tf_op jit(solution)/shard_map/all_to_all | solution.py:15
  319.0 10.4 %slice_bitcast_fusion = (bf16[16,512,384]{1,2,0:T(8,128)(2,1)}, bf16[16,512,384]{1,2,0:T(8,128)(2,1)}) fusion(bf16[2,16,512,384]{2,3,0,1:T(8,128)(2,1)} %bitcast.2), kind=kLoop, calls=%fused_computation.21 | loop fusion | bytes 25165824 | tf_op jit(solution)/shard_map/reshape;squeeze | solution.py:57
  329.5 152.1 %while.15 = (s32[]{:T(128)}, f32[3,512]{1,0:T(4,128)S(1)}, f32[3,512]{1,0:T(4,128)S(1)}, f32[3,512,128]{2,1,0:T(8,128)}, s32[4,12]{0,1:T(8,128)S(1)}, /*index=5*...) while((s32[]{:T(128)}, f32[3,512]{1,0:T(4,128)S(1)}, ...), condition=%wide.region_8.9_spmd.clone, body=%wide.region_4.8_spmd.clone.sunk | while | flops 413521408 | bytes 23312788 | solution.py:64
  329.8 1.6 broadcast_in_dim.85
  331.5 1.9 constant_dynamic-slice_fusion.7
  333.4 1.8 fusion.38
  339.3 1.6 broadcast_in_dim.85
  341.0 1.9 constant_dynamic-slice_fusion.7
  342.9 1.8 fusion.38
  348.8 1.6 broadcast_in_dim.85
  350.5 1.9 constant_dynamic-slice_fusion.7
  352.4 1.8 fusion.38
  360.0 1.9 constant_dynamic-slice_fusion.7
  361.9 1.9 fusion.38
  369.5 1.9 constant_dynamic-slice_fusion.7
  371.4 1.8 fusion.38
  377.3 1.6 broadcast_in_dim.85
  379.0 1.9 constant_dynamic-slice_fusion.7
  380.9 1.8 fusion.38
  386.8 1.6 broadcast_in_dim.85
  388.5 1.9 constant_dynamic-slice_fusion.7
  390.5 1.8 fusion.38
  396.3 1.6 broadcast_in_dim.85
  398.0 1.9 constant_dynamic-slice_fusion.7
  400.0 1.9 fusion.38
  405.8 1.6 broadcast_in_dim.85
  407.6 1.9 constant_dynamic-slice_fusion.7
  409.5 1.8 fusion.38
  415.3 1.6 broadcast_in_dim.85
  417.1 1.9 constant_dynamic-slice_fusion.7
  419.0 1.8 fusion.38
  426.6 1.9 constant_dynamic-slice_fusion.7
  428.5 1.8 fusion.38
  434.3 1.6 broadcast_in_dim.85
  436.1 1.9 constant_dynamic-slice_fusion.7
  438.0 1.9 fusion.38
  443.8 1.6 broadcast_in_dim.85
  445.6 1.9 constant_dynamic-slice_fusion.7
  447.5 1.8 fusion.38
  455.1 1.9 constant_dynamic-slice_fusion.7
  457.0 1.8 fusion.38
  464.6 1.9 constant_dynamic-slice_fusion.7
  466.5 1.8 fusion.38
  474.1 1.9 constant_dynamic-slice_fusion.7
  476.0 1.9 fusion.38
  (267 shorter events, 83.3 us)
Async XLA Ops:
  0.0 50.8 %copy-start = (s32[64,12]{0,1:T(8,128)S(1)}, s32[64,12]{0,1:T(8,128)}, u32[]{:S(2)}) copy-start(s32[64,12]{0,1:T(8,128)} %param.13) | copy-start | bytes 9220
  42.3 7.5 %copy-start.4 = (f32[384]{0:T(512)S(1)}, f32[384]{0:T(512)}, u32[]{:S(2)}) copy-start(f32[384]{0:T(512)} %param.11) | copy-start | bytes 4612
  42.3 276.8 %all-to-all-start = ((bf16[16,2,512,384]{2,3,1,0:T(8,128)(2,1)}), bf16[16,2,512,384]{2,3,1,0:T(8,128)(2,1)}, u32[]{:S(2)}, u32[]{:S(2)}) async-start(bf16[16,2,512,384]{2,3,1,0:T(8,128)(2,1)} %stack.11), calls=%async_computation | async-start | bytes 25165824 | tf_op jit(solution)/shard_map/all_to_all | solution.py:15
  335.3 1.0 copy-start.1
  335.3 1.2 copy-start.2
  338.0 0.9 copy-start.3
  344.8 1.0 copy-start.1
  344.8 1.2 copy-start.2
  347.5 0.9 copy-start.3
  354.3 1.0 copy-start.1
  354.3 1.2 copy-start.2
  357.0 0.9 copy-start.3
  363.8 1.0 copy-start.1
  363.8 1.2 copy-start.2
  366.5 0.9 copy-start.3
  373.3 1.0 copy-start.1
  373.3 1.2 copy-start.2
  376.0 0.9 copy-start.3
  382.8 1.0 copy-start.1
  382.8 1.2 copy-start.2
  385.5 0.9 copy-start.3
  392.3 1.0 copy-start.1
  392.3 1.2 copy-start.2
  395.0 0.9 copy-start.3
  401.8 1.0 copy-start.1
  401.8 1.2 copy-start.2
  404.6 0.9 copy-start.3
  411.3 1.0 copy-start.1
  411.3 1.2 copy-start.2
  414.1 0.9 copy-start.3
  420.8 1.0 copy-start.1
  420.8 1.2 copy-start.2
  423.6 0.9 copy-start.3
  430.3 1.0 copy-start.1
  430.3 1.2 copy-start.2
  433.1 0.9 copy-start.3
  439.8 1.0 copy-start.1
  439.8 1.2 copy-start.2
  442.6 0.9 copy-start.3
  449.3 1.0 copy-start.1
  449.4 1.2 copy-start.2
  458.8 1.0 copy-start.1
  458.9 1.2 copy-start.2
  461.6 0.9 copy-start.3
  468.4 1.0 copy-start.1
  468.4 1.2 copy-start.2
  477.9 1.0 copy-start.1
  477.9 1.2 copy-start.2
  (3 other events, 2.8 us)
